TPU v7x, 32 devices: a whole 2x2x4 slice. The times are simulated.
32 devices in a mesh: rep: 2 (over y), seq: 4 (over z), head: 4 (over x, core).
Axes of the slice: x: 2, y: 2, z: 4, core: 2. Of those that a mesh axis runs over, the one named last changes fastest.
Arguments:
- queries: bfloat16 [3072, 2560], P(('rep', 'seq'), 'head'), parts along dimension 0, may hold values from -16 to 16
- keys: bfloat16 [3072, 2560], P(('rep', 'seq'), 'head'), parts along dimension 0, may hold values from -6 to 6
- values: bfloat16 [3072, 2560], P(('rep', 'seq'), 'head'), parts along dimension 0, may hold values from -6 to 6
- out_weight: bfloat16 [2560, 5120], P('seq', 'head'), may hold values from -0.3125 to 0.3125
- neighbours: int32 [8, 27], P('rep'), parts along dimension 0, may hold values from -1 to 3, as said below
- clip_ids: int32 [3072], P(('rep', 'seq')), parts along dimension 0, may hold values from 0 to 1
Outputs:
- output: bfloat16 [3072, 5120], P(('rep', 'seq'), 'head'), parts along dimension 0
There are 2 independent parts, one for each index of `rep`. A program takes and returns all parts, laid end to end along the dimension named above; an argument that names none is the same for every part. Nothing has to cross between parts.
Inputs may be any that keep to these rules, and one draw needn't show every extreme that they name: `neighbours`: column 9 (a + 1) + 3 (b + 1) + (c + 1) of row s, for a, b, c each -1, 0 or 1, is either -1 or s + a * 4 * 7 + b * 7 + c; column 13 of row s is s.
All inputs are finite; a program needn't handle non-finite values.
Results may differ from a plain program's by a relative error of at most 0.0058.
Values may be sent and summed in bfloat16 or wider, within the bound.
No kernel may reach another device: no remote copies, remote signals or barrier semaphores. Data moves between devices by JAX's collectives and lax.ppermute only.
A program may use at most 192 MiB of HBM per device.

v0:
```python
import math
import jax
import jax.numpy as jnp
from jax import lax
from jax.sharding import PartitionSpec as P

HD = 128
TGH = 4
TGW = 7


def from_behind(value, axis, by):
    peers = lax.axis_size(axis)
    pairs = [(i, i + by) for i in range(peers) if 0 <= i + by < peers]
    return lax.ppermute(value, axis, pairs)


def attend_head(query_head, key_head, value_head, allowed):
    scores = lax.dot_general(
        query_head, key_head, (((1,), (1,)), ((), ())), preferred_element_type=jnp.float32
    ) * (1.0 / math.sqrt(query_head.shape[1]))
    masked = jnp.where(allowed, scores, -1e30)
    highest = jnp.max(masked, axis=1, keepdims=True)
    raised = jnp.where(allowed, jnp.exp(masked - highest), 0.0)
    summed = jnp.sum(raised, axis=1, keepdims=True)
    weights = (raised / summed).astype(jnp.bfloat16)
    return jnp.dot(weights, value_head, preferred_element_type=jnp.float32).astype(jnp.bfloat16)


def on_device(queries, keys, values, out_weight, neighbours, clip_ids):
    tile_rows = queries.shape[0]
    feature_width = queries.shape[1]
    seq_count = lax.axis_size("seq")
    layer_tiles = TGH * TGW
    every_offset = set()
    for layer_step in (-1, 0, 1):
        for row_step in (-1, 0, 1):
            for col_step in (-1, 0, 1):
                every_offset.add(layer_step * layer_tiles + row_step * TGW + col_step)
    distances = [offset for offset in sorted(every_offset) if 0 < offset < seq_count]
    key_list = [keys]
    value_list = [values]
    clip_list = [clip_ids]
    offsets = [0]
    for distance in distances:
        below_keys, below_values, below_clips = from_behind(
            (keys, values, clip_ids), "seq", distance
        )
        above_keys, above_values, above_clips = from_behind(
            (keys, values, clip_ids), "seq", -distance
        )
        key_list += [below_keys, above_keys]
        value_list += [below_values, above_values]
        clip_list += [below_clips, above_clips]
        offsets += [distance, -distance]
    key_stack = jnp.stack(key_list)
    value_stack = jnp.stack(value_list)
    clip_stack = jnp.stack(clip_list)
    blocks = key_stack.shape[0]
    position = lax.axis_index("seq")
    window_row = lax.dynamic_index_in_dim(neighbours, position, 0, keepdims=False)
    sources = position - jnp.asarray(offsets, dtype=jnp.int32)
    present = jnp.any(
        (window_row[None, :] == sources[:, None]) & (window_row[None, :] >= 0), axis=1
    )
    key_clips = clip_stack.reshape(blocks * tile_rows)
    allowed = jnp.repeat(present, tile_rows)[None, :] & (clip_ids[:, None] == key_clips[None, :])
    key_rows = key_stack.reshape(blocks * tile_rows, feature_width)
    value_rows = value_stack.reshape(blocks * tile_rows, feature_width)
    head_outputs = []
    for head_index in range(feature_width // HD):
        first_col = head_index * HD
        head_outputs.append(
            attend_head(
                queries[:, first_col : first_col + HD],
                key_rows[:, first_col : first_col + HD],
                value_rows[:, first_col : first_col + HD],
                allowed,
            )
        )
    attended = jnp.concatenate(head_outputs, axis=1)
    all_features = lax.all_gather(attended, "head", axis=1, tiled=True)
    empty = jnp.zeros((tile_rows, out_weight.shape[1]), jnp.float32)
    weight_piece = lax.all_gather(out_weight, "seq", axis=0, tiled=True)
    features = lax.slice_in_dim(all_features, 0, weight_piece.shape[0], axis=1)
    projected = empty + jnp.dot(features, weight_piece, preferred_element_type=jnp.float32)
    return projected.astype(jnp.bfloat16)


def solution(mesh):
    in_specs = (
        P(("rep", "seq"), "head"),
        P(("rep", "seq"), "head"),
        P(("rep", "seq"), "head"),
        P("seq", "head"),
        P("rep", None),
        P(("rep", "seq")),
    )
    out_specs = P(("rep", "seq"), "head")
    return jax.shard_map(
        on_device, mesh=mesh, in_specs=in_specs, out_specs=out_specs, check_vma=False
    )
```

profile of v0, /device:TPU:0, one launch (start us, length us, event | category | flops | bytes accessed | tf_op | source)
XLA Modules:
  0.0 208.0 jit_solution(14518805611755408136)
XLA Ops:
  6.5 0.0 copy-start.2
  6.5 0.0 copy-start.3
  6.5 0.0 all-gather.3.cloned.1.call-start
  6.5 5.0 %collective-permute-start = (s32[384]{0:T(512)}, s32[384]{0:T(512)S(1)}, u32[]{:S(2)}, u32[]{:S(2)}) collective-permute-start(s32[384]{0:T(512)} %param.12), channel_id=1, source_target_pairs={{0,4},{4,8},{8,12},{1,5},{5,9},{9,13},{2,6},{6,10},{10,14},{3,7},{... | collective-permute-start | bytes 4616 | tf_op jit(solution)/shard_map/ppermute | solution.py:15
  11.6 1.3 collective-permute-start.1
  12.9 4.6 %collective-permute-start.2 = (bf16[384,640]{1,0:T(8,128)(2,1)}, bf16[384,640]{1,0:T(8,128)(2,1)S(1)}, u32[]{:S(2)}, u32[]{:S(2)}) collective-permute-start(bf16[384,640]{1,0:T(8,128)(2,1)} %param.8), channel_id=1, source_target_pairs={{0,4},{4,8},{8,12},{1,5},{5,9},{9,13},{2,6},{6,10},{10,14},{3,7},{... | collective-permute-start | bytes 1474568 | tf_op jit(solution)/shard_map/ppermute | solution.py:15
  17.5 1.3 collective-permute-start.3
  18.8 4.6 %collective-permute-start.4 = (bf16[384,640]{1,0:T(8,128)(2,1)}, bf16[384,640]{1,0:T(8,128)(2,1)S(1)}, u32[]{:S(2)}, u32[]{:S(2)}) collective-permute-start(bf16[384,640]{1,0:T(8,128)(2,1)} %param.9), channel_id=1, source_target_pairs={{0,4},{4,8},{8,12},{1,5},{5,9},{9,13},{2,6},{6,10},{10,14},{3,7},{... | collective-permute-start | bytes 1474568 | tf_op jit(solution)/shard_map/ppermute | solution.py:15
  23.4 0.7 compare_bitcast_fusion
  24.1 0.7 fusion.35
  24.8 0.7 broadcast_add_fusion
  25.4 0.2 and_reduce_fusion
  25.6 0.7 stack.36
  26.3 0.1 broadcast_in_dim.32
  26.4 0.0 collective-permute-done
  26.4 1.3 collective-permute-start.5
  27.7 0.0 collective-permute-done.1
  27.8 1.7 collective-permute-done.2
  29.4 4.3 %collective-permute-done.3 = bf16[384,640]{1,0:T(8,128)(2,1)S(1)} collective-permute-done((bf16[384,640]{1,0:T(8,128)(2,1)}, bf16[384,640]{1,0:T(8,128)(2,1)S(1)}, u32[]{:S(2)}, u32[]{:S(2)}) %collective-permute-start.3) | collective-permute-done | bytes 491552 | tf_op jit(solution)/shard_map/ppermute | solution.py:15
  33.8 1.2 pad_maximum_fusion
  35.0 0.0 copy-done.2
  35.0 0.0 copy-done.3
  35.0 0.6 fusion.41
  35.6 0.6 fusion.42
  36.3 0.6 fusion.43
  36.9 0.6 fusion.44
  37.5 0.0 copy-start
  37.5 0.6 fusion.45
  38.2 0.1 collective-permute-done.4
  38.2 4.0 %collective-permute-done.5 = bf16[384,640]{1,0:T(8,128)(2,1)S(1)} collective-permute-done((bf16[384,640]{1,0:T(8,128)(2,1)}, bf16[384,640]{1,0:T(8,128)(2,1)S(1)}, u32[]{:S(2)}, u32[]{:S(2)}) %collective-permute-start.5) | collective-permute-done | bytes 491552 | tf_op jit(solution)/shard_map/ppermute | solution.py:15
  42.2 0.0 copy-done
  42.3 0.2 pad_maximum_fusion.1
  42.4 2.3 %fusion.14 = (f32[384]{0:T(512)S(1)}, f32[384]{0:T(512)S(1)}, f32[384]{0:T(512)S(1)}, f32[384]{0:T(512)S(1)}, f32[384]{0:T(512)S(1)}) fusion(f32[384,1152]{0,1:T(8,128)S(1)} %get-tuple-element.11, f32[384]{0:T(512)S(1)} %get-tuple-element.10, s32[384]{0:T(512)S(1)} %copy-done.2, s32[1152]{0:T(1024)S(1)} %eq.35, pred[1152]{0:T(1024)(128)(4,1)S(1)} %and.24, ...), kind=kLoop, calls=%fused_computation.33 | loop fusion | flops 7518336 | bytes 8870016 | tf_op jit(solution)/shard_map/reduce_sum | solution.py:25
  44.7 1.0 fusion.15
  45.7 1.0 fusion.16
  46.8 1.0 fusion.17
  47.8 1.0 fusion.18
  48.8 1.0 fusion.19
  49.8 0.0 copy-start.1
  49.8 0.8 copy-done.1
  50.6 0.0 all-gather.3.cloned.1.call-update
  50.6 0.0 all-gather.5.cloned.1.call-start
  50.7 0.7 all-gather.5.cloned.1.call-update
  51.4 21.5 %all-gather.3.cloned.1.call-done = bf16[384,2560]{1,0:T(8,128)(2,1)} async-done(((bf16[384,640]{1,0:T(8,128)(2,1)}), bf16[384,2560]{1,0:T(8,128)(2,1)}) %all-gather.3.cloned.1.call-update) | async-done | bytes 1966096 | tf_op jit(solution)/shard_map/all_gather | solution.py:82
  72.8 121.2 %all-gather.5.cloned.1.call-done = bf16[2560,1280]{1,0:T(8,128)(2,1)} async-done(((bf16[640,1280]{1,0:T(8,128)(2,1)}), bf16[2560,1280]{1,0:T(8,128)(2,1)}) %all-gather.5.cloned.1.call-update) | async-done | bytes 6553616 | tf_op jit(solution)/shard_map/all_gather | solution.py:84
  194.1 7.1 %convolution_convert_fusion = bf16[384,1280]{1,0:T(8,128)(2,1)} fusion(bf16[384,2560]{1,0:T(8,128)(2,1)} %all-gather.3.cloned.1.call-done, bf16[2560,1280]{1,0:T(8,128)(2,1)} %all-gather.5.cloned.1.call-done), kind=kOutput, calls=%fused_computation.15 | convolution fusion | flops 2517073920 | bytes 9502720 | tf_op jit(solution)/shard_map/dot_general | solution.py:86
  (5 shorter events, 0.0 us)
Async XLA Ops:
  6.5 28.4 %copy-start.2 = (s32[384]{0:T(512)S(1)}, s32[384]{0:T(512)}, u32[]{:S(2)}) copy-start(s32[384]{0:T(512)} %param.12) | copy-start | bytes 4612
  6.5 28.5 %copy-start.3 = (bf16[384,640]{1,0:T(8,128)(2,1)S(1)}, bf16[384,640]{1,0:T(8,128)(2,1)}, u32[]{:S(2)}) copy-start(bf16[384,640]{1,0:T(8,128)(2,1)} %param.7) | copy-start | bytes 1474564
  6.5 66.3 %all-gather.3.cloned.1.call-start = ((), (), s32[]{:S(2)}) async-start(), calls=%async_computation | async-start | bytes 2457600 | tf_op jit(solution)/shard_map/all_gather | solution.py:82
  6.5 19.8 %collective-permute-start = (s32[384]{0:T(512)}, s32[384]{0:T(512)S(1)}, u32[]{:S(2)}, u32[]{:S(2)}) collective-permute-start(s32[384]{0:T(512)} %param.12), channel_id=1, source_target_pairs={{0,4},{4,8},{8,12},{1,5},{5,9},{9,13},{2,6},{6,10},{10,14},{3,7},{... | collective-permute-start | bytes 4616 | tf_op jit(solution)/shard_map/ppermute | solution.py:15
  11.6 16.1 %collective-permute-start.1 = (s32[384]{0:T(512)}, s32[384]{0:T(512)S(1)}, u32[]{:S(2)}, u32[]{:S(2)}) collective-permute-start(s32[384]{0:T(512)} %param.12), channel_id=1, source_target_pairs={{4,0},{8,4},{12,8},{5,1},{9,5},{13,9},{6,2},{10,6},{14,10},{7,3},{... | collective-permute-start | bytes 4616 | tf_op jit(solution)/shard_map/ppermute | solution.py:15
  12.9 16.5 %collective-permute-start.2 = (bf16[384,640]{1,0:T(8,128)(2,1)}, bf16[384,640]{1,0:T(8,128)(2,1)S(1)}, u32[]{:S(2)}, u32[]{:S(2)}) collective-permute-start(bf16[384,640]{1,0:T(8,128)(2,1)} %param.8), channel_id=1, source_target_pairs={{0,4},{4,8},{8,12},{1,5},{5,9},{9,13},{2,6},{6,10},{10,14},{3,7},{... | collective-permute-start | bytes 1474568 | tf_op jit(solution)/shard_map/ppermute | solution.py:15
  17.5 16.3 %collective-permute-start.3 = (bf16[384,640]{1,0:T(8,128)(2,1)}, bf16[384,640]{1,0:T(8,128)(2,1)S(1)}, u32[]{:S(2)}, u32[]{:S(2)}) collective-permute-start(bf16[384,640]{1,0:T(8,128)(2,1)} %param.8), channel_id=1, source_target_pairs={{4,0},{8,4},{12,8},{5,1},{9,5},{13,9},{6,2},{10,6},{14,10},{7,3},{... | collective-permute-start | bytes 1474568 | tf_op jit(solution)/shard_map/ppermute | solution.py:15
  18.8 19.4 %collective-permute-start.4 = (bf16[384,640]{1,0:T(8,128)(2,1)}, bf16[384,640]{1,0:T(8,128)(2,1)S(1)}, u32[]{:S(2)}, u32[]{:S(2)}) collective-permute-start(bf16[384,640]{1,0:T(8,128)(2,1)} %param.9), channel_id=1, source_target_pairs={{0,4},{4,8},{8,12},{1,5},{5,9},{9,13},{2,6},{6,10},{10,14},{3,7},{... | collective-permute-start | bytes 1474568 | tf_op jit(solution)/shard_map/ppermute | solution.py:15
  26.4 15.9 %collective-permute-start.5 = (bf16[384,640]{1,0:T(8,128)(2,1)}, bf16[384,640]{1,0:T(8,128)(2,1)S(1)}, u32[]{:S(2)}, u32[]{:S(2)}) collective-permute-start(bf16[384,640]{1,0:T(8,128)(2,1)} %param.9), channel_id=1, source_target_pairs={{4,0},{8,4},{12,8},{5,1},{9,5},{13,9},{6,2},{10,6},{14,10},{7,3},{... | collective-permute-start | bytes 1474568 | tf_op jit(solution)/shard_map/ppermute | solution.py:15
  37.5 4.7 %copy-start = (bf16[384,640]{1,0:T(8,128)(2,1)S(1)}, bf16[384,640]{1,0:T(8,128)(2,1)}, u32[]{:S(2)}) copy-start(bf16[384,640]{1,0:T(8,128)(2,1)} %param.9) | copy-start | bytes 1474564
  49.8 0.8 copy-start.1
  50.6 143.4 %all-gather.5.cloned.1.call-start = ((), (), s32[]{:S(2)}) async-start(), calls=%async_computation.1 | async-start | bytes 8192000 | tf_op jit(solution)/shard_map/all_gather | solution.py:84
Sparse Core Ops, SparseCore 0:
  50.7 22.0 all-gather.2
  74.4 119.6 all-gather.4
where the time goes:
time: 208 us
  waiting for transfers between devices  154 us (74%)
  starting transfers between devices  18.1 us (9%)
  matrix products  15.3 us (7%)
  between operations  13.6 us (7%)
  other arithmetic  5.25 us (3%)
  local copies, waits for them, and re-layouts  2.27 us (1%)
    all_gather x1, waiting for transfers between devices, on_device(): weight_piece = lax.all_gather(out_weight, 'seq', axis=0, tiled=True)  121 us
    all_gather x1, waiting for transfers between devices, on_device(): all_features = lax.all_gather(attended, 'head', axis=1, tiled=True)  21.5 us
    ppermute x6, starting transfers between devices, from_behind(): return lax.ppermute(value, axis, pairs)  18.1 us
    ppermute x6, waiting for transfers between devices, from_behind(): return lax.ppermute(value, axis, pairs)  10.1 us
    dot_general x1, matrix products, on_device(): jnp.dot(features, weight_piece, preferred_element_type=jnp.float32)  7.1 us
    dot_general x5, matrix products, attend_head(): jnp.dot(weights, value_head, preferred_element_type=jnp.float32)  5.04 us
  transfers between devices with their start and end apart: 8, of which 6 were waited for; matrix products, arithmetic and copies ran while one was open for 4% of the time, Pallas kernels for 0%

commit v1 on v0

--- a/solution.py
+++ b/solution.py
@@ -79,7 +79,12 @@
             )
         )
     attended = jnp.concatenate(head_outputs, axis=1)
-    all_features = lax.all_gather(attended, "head", axis=1, tiled=True)
+    ring = [attended]
+    for hop in range(3):
+        ring.append(lax.ppermute(ring[-1], "head", [(dev, (dev + 1) % 4) for dev in range(4)]))
+    all_features = jnp.roll(
+        jnp.concatenate(ring[::-1], axis=1), (lax.axis_index("head") + 1) * ring[0].shape[1], axis=1
+    )
     empty = jnp.zeros((tile_rows, out_weight.shape[1]), jnp.float32)
     weight_piece = lax.all_gather(out_weight, "seq", axis=0, tiled=True)
     features = lax.slice_in_dim(all_features, 0, weight_piece.shape[0], axis=1)

time: 208 us -> 159 us (0.76)
  waiting for transfers between devices: 154 us -> 94 us
  local copies, waits for them, and re-layouts: 2.27 us -> 13.8 us
    all_gather x1, waiting for transfers between devices: 121 us -> 28.9 us  [on_device(): weight_piece = lax.all_gather(out_weight, 'seq', axis=0, tiled=True)]
    ppermute x6, waiting for transfers between devices: 10.1 us -> 39.6 us  [from_behind(): return lax.ppermute(value, axis, pairs)]
    ppermute x0 -> x3, waiting for transfers between devices: none -> 24.7 us  [on_device(): lax.ppermute(ring[-1], 'head', [(dev, (dev + 1) % 4) for dev in range(4)])]
    all_gather x1 -> x0, waiting for transfers between devices: 21.5 us -> none  [on_device(): all_features = lax.all_gather(attended, 'head', axis=1, tiled=True)]
    unnamed x8 -> x23, local copies, waits for them, and re-layouts: 0.79 us -> 11.7 us
  transfers between devices with their start and end apart: 8 -> 10, of which waited for: 6 -> 6; matrix products, arithmetic and copies ran while one was open for 4% -> 16% of each run, Pallas kernels for 0% -> 0%
where the time goes in v1:
time: 159 us
  waiting for transfers between devices  94 us (59%)
  starting transfers between devices  18.1 us (11%)
  matrix products  14.9 us (9%)
  local copies, waits for them, and re-layouts  13.8 us (9%)
  between operations  13.6 us (9%)
  other arithmetic  4.24 us (3%)
    ppermute x6, waiting for transfers between devices, from_behind(): return lax.ppermute(value, axis, pairs)  39.6 us
    all_gather x1, waiting for transfers between devices, on_device(): weight_piece = lax.all_gather(out_weight, 'seq', axis=0, tiled=True)  28.9 us
    ppermute x3, waiting for transfers between devices, on_device(): lax.ppermute(ring[-1], 'head', [(dev, (dev + 1) % 4) for dev in range(4)])  24.7 us
    ppermute x6, starting transfers between devices, from_behind(): return lax.ppermute(value, axis, pairs)  18.1 us
    unnamed x23, local copies, waits for them, and re-layouts  11.7 us
    dot_general x1, matrix products, on_device(): jnp.dot(features, weight_piece, preferred_element_type=jnp.float32)  7.17 us
    dot_general x5, matrix products, attend_head(): jnp.dot(weights, value_head, preferred_element_type=jnp.float32)  4.62 us
  transfers between devices with their start and end apart: 10, of which 6 were waited for; matrix products, arithmetic and copies ran while one was open for 16% of the time, Pallas kernels for 0%

profile of v1, /device:TPU:0, one launch (start us, length us, event | category | flops | bytes accessed | tf_op | source)
XLA Modules:
  0.0 158.7 jit_solution(13809563600175920477)
XLA Ops:
  6.5 0.0 all-gather.2.cloned.1.call-start
  6.5 0.7 all-gather.2.cloned.1.call-update
  7.3 0.0 copy-start.1
  7.3 5.1 %collective-permute-start.2 = (bf16[384,640]{1,0:T(8,128)(2,1)}, bf16[384,640]{1,0:T(8,128)(2,1)S(1)}, u32[]{:S(2)}, u32[]{:S(2)}) collective-permute-start(bf16[384,640]{1,0:T(8,128)(2,1)} %param.8), channel_id=1, source_target_pairs={{0,4},{4,8},{8,12},{1,5},{5,9},{9,13},{2,6},{6,10},{10,14},{3,7},{... | collective-permute-start | bytes 1474568 | tf_op jit(solution)/shard_map/ppermute | solution.py:15
  12.4 1.3 collective-permute-start.3
  13.7 4.6 %collective-permute-start.4 = (bf16[384,640]{1,0:T(8,128)(2,1)}, bf16[384,640]{1,0:T(8,128)(2,1)S(1)}, u32[]{:S(2)}, u32[]{:S(2)}) collective-permute-start(bf16[384,640]{1,0:T(8,128)(2,1)} %param.9), channel_id=1, source_target_pairs={{0,4},{4,8},{8,12},{1,5},{5,9},{9,13},{2,6},{6,10},{10,14},{3,7},{... | collective-permute-start | bytes 1474568 | tf_op jit(solution)/shard_map/ppermute | solution.py:15
  18.2 1.3 collective-permute-start.5
  19.5 4.5 %collective-permute-start = (s32[384]{0:T(512)}, s32[384]{0:T(512)S(1)}, u32[]{:S(2)}, u32[]{:S(2)}) collective-permute-start(s32[384]{0:T(512)} %param.12), channel_id=1, source_target_pairs={{0,4},{4,8},{8,12},{1,5},{5,9},{9,13},{2,6},{6,10},{10,14},{3,7},{... | collective-permute-start | bytes 4616 | tf_op jit(solution)/shard_map/ppermute | solution.py:15
  24.1 0.7 broadcast_add_fusion
  24.8 0.7 compare_bitcast_fusion
  25.5 0.7 fusion.32
  26.1 21.0 %collective-permute-done = s32[384]{0:T(512)S(1)} collective-permute-done((s32[384]{0:T(512)}, s32[384]{0:T(512)S(1)}, u32[]{:S(2)}, u32[]{:S(2)}) %collective-permute-start) | collective-permute-done | bytes 1568 | tf_op jit(solution)/shard_map/ppermute | solution.py:15
  47.1 1.3 collective-permute-start.1
  48.4 0.2 and_reduce_fusion
  48.6 0.7 stack.36
  49.3 0.1 broadcast_in_dim.32
  49.4 18.6 %collective-permute-done.1 = s32[384]{0:T(512)S(1)} collective-permute-done((s32[384]{0:T(512)}, s32[384]{0:T(512)S(1)}, u32[]{:S(2)}, u32[]{:S(2)}) %collective-permute-start.1) | collective-permute-done | bytes 1568 | tf_op jit(solution)/shard_map/ppermute | solution.py:15
  68.0 0.0 collective-permute-done.2
  68.0 0.0 collective-permute-done.3
  68.0 0.0 copy-done
  68.0 0.2 pad_maximum_fusion
  68.2 0.0 copy-start.2
  68.3 0.0 copy-start.3
  68.3 0.0 collective-permute-done.4
  68.3 0.0 collective-permute-done.5
  68.3 0.0 copy-done.1
  68.3 0.2 pad_maximum_fusion.1
  68.5 0.4 copy-done.2
  68.9 0.4 copy-done.3
  69.3 0.6 fusion.38
  69.9 0.6 fusion.39
  70.6 0.6 fusion.40
  71.2 0.6 fusion.41
  71.8 0.6 fusion.42
  72.5 2.3 %fusion.15 = (f32[384]{0:T(512)S(1)}, f32[384]{0:T(512)S(1)}, f32[384]{0:T(512)S(1)}, f32[384]{0:T(512)S(1)}, f32[384]{0:T(512)S(1)}) fusion(f32[384,1152]{0,1:T(8,128)S(1)} %get-tuple-element.11, f32[384]{0:T(512)S(1)} %get-tuple-element.10, s32[384]{0:T(512)S(1)} %copy-done.2, s32[1152]{0:T(1024)S(1)} %eq.38, pred[1152]{0:T(1024)(128)(4,1)S(1)} %and.30, ...), kind=kLoop, calls=%fused_computation.34 | loop fusion | flops 7518336 | bytes 8870016 | tf_op jit(solution)/shard_map/reduce_sum | solution.py:25
  74.8 0.9 constant_dynamic-update-slice_fusion.4
  75.7 0.9 constant_dynamic-update-slice_fusion.3
  76.6 0.9 constant_dynamic-update-slice_fusion.2
  77.6 0.9 constant_dynamic-update-slice_fusion.1
  78.5 0.9 constant_dynamic-update-slice_fusion
  79.4 0.1 collective-permute-start.6
  79.5 8.2 %collective-permute-done.6 = bf16[384,640]{0,1:T(8,128)(2,1)S(1)} collective-permute-done((bf16[384,640]{0,1:T(8,128)(2,1)S(1)}, bf16[384,640]{0,1:T(8,128)(2,1)S(1)}, u32[]{:S(2)}, u32[]{:S(2)}) %collective-permute-start.6) | collective-permute-done | bytes 491552 | tf_op jit(solution)/shard_map/ppermute | solution.py:84
  87.7 0.0 collective-permute-start.7
  87.7 8.3 %collective-permute-done.7 = bf16[384,640]{0,1:T(8,128)(2,1)S(1)} collective-permute-done((bf16[384,640]{0,1:T(8,128)(2,1)S(1)}, bf16[384,640]{0,1:T(8,128)(2,1)S(1)}, u32[]{:S(2)}, u32[]{:S(2)}) %collective-permute-start.7) | collective-permute-done | bytes 491552 | tf_op jit(solution)/shard_map/ppermute | solution.py:84
  96.0 0.0 collective-permute-start.8
  96.0 8.3 %collective-permute-done.8 = bf16[384,640]{0,1:T(8,128)(2,1)S(1)} collective-permute-done((bf16[384,640]{0,1:T(8,128)(2,1)S(1)}, bf16[384,640]{0,1:T(8,128)(2,1)S(1)}, u32[]{:S(2)}, u32[]{:S(2)}) %collective-permute-start.8) | collective-permute-done | bytes 491552 | tf_op jit(solution)/shard_map/ppermute | solution.py:84
  104.2 0.8 constant_dynamic-update-slice_fusion.20
  105.1 0.8 constant_dynamic-update-slice_fusion.19
  105.9 0.8 constant_dynamic-update-slice_fusion.18
  106.7 0.6 constant_dynamic-update-slice_fusion.17
  107.4 0.7 constant_dynamic-update-slice_fusion.16
  108.0 0.6 constant_dynamic-update-slice_fusion.15
  108.7 0.7 constant_dynamic-update-slice_fusion.14
  109.3 0.6 constant_dynamic-update-slice_fusion.13
  110.0 0.9 constant_dynamic-update-slice_fusion.12
  110.8 0.9 constant_dynamic-update-slice_fusion.11
  111.7 0.8 constant_dynamic-update-slice_fusion.10
  112.5 0.6 constant_dynamic-update-slice_fusion.9
  113.2 0.6 constant_dynamic-update-slice_fusion.8
  113.8 0.6 constant_dynamic-update-slice_fusion.7
  114.5 0.6 constant_dynamic-update-slice_fusion.6
  115.1 0.6 constant_dynamic-update-slice_fusion.5
  115.8 28.9 %all-gather.2.cloned.1.call-done = bf16[2560,1280]{1,0:T(8,128)(2,1)} async-done(((bf16[640,1280]{1,0:T(8,128)(2,1)}), bf16[2560,1280]{1,0:T(8,128)(2,1)}) %all-gather.2.cloned.1.call-update) | async-done | bytes 6553616 | tf_op jit(solution)/shard_map/all_gather | solution.py:89
  144.7 7.2 %convolution_convert_fusion = bf16[384,1280]{1,0:T(8,128)(2,1)} fusion(bf16[2560,1280]{1,0:T(8,128)(2,1)} %all-gather.2.cloned.1.call-done, bf16[384,5120]{0,1:T(8,128)(2,1)} %constant_dynamic-update-slice_fusion.5, s32[]{:T(128)S(6)} %select_n.60), kind=kOutput, calls=%fused_computation.15 | convolution fusion | flops 2517073920 | bytes 9502724 | tf_op jit(solution)/shard_map/dot_general | solution.py:91
  (6 shorter events, 0.1 us)
Async XLA Ops:
  6.5 61.5 %copy-start = (bf16[384,640]{1,0:T(8,128)(2,1)S(1)}, bf16[384,640]{1,0:T(8,128)(2,1)}, u32[]{:S(2)}) copy-start(bf16[384,640]{1,0:T(8,128)(2,1)} %param.8) | copy-start | bytes 1474564
  6.5 138.2 %all-gather.2.cloned.1.call-start = ((), (), s32[]{:S(2)}) async-start(), calls=%async_computation | async-start | bytes 8192000 | tf_op jit(solution)/shard_map/all_gather | solution.py:89
  7.3 61.0 %copy-start.1 = (bf16[384,640]{1,0:T(8,128)(2,1)S(1)}, bf16[384,640]{1,0:T(8,128)(2,1)}, u32[]{:S(2)}) copy-start(bf16[384,640]{1,0:T(8,128)(2,1)} %param.9) | copy-start | bytes 1474564
  7.3 60.8 %collective-permute-start.2 = (bf16[384,640]{1,0:T(8,128)(2,1)}, bf16[384,640]{1,0:T(8,128)(2,1)S(1)}, u32[]{:S(2)}, u32[]{:S(2)}) collective-permute-start(bf16[384,640]{1,0:T(8,128)(2,1)} %param.8), channel_id=1, source_target_pairs={{0,4},{4,8},{8,12},{1,5},{5,9},{9,13},{2,6},{6,10},{10,14},{3,7},{... | collective-permute-start | bytes 1474568 | tf_op jit(solution)/shard_map/ppermute | solution.py:15
  12.4 55.7 %collective-permute-start.3 = (bf16[384,640]{1,0:T(8,128)(2,1)}, bf16[384,640]{1,0:T(8,128)(2,1)S(1)}, u32[]{:S(2)}, u32[]{:S(2)}) collective-permute-start(bf16[384,640]{1,0:T(8,128)(2,1)} %param.8), channel_id=1, source_target_pairs={{4,0},{8,4},{12,8},{5,1},{9,5},{13,9},{6,2},{10,6},{14,10},{7,3},{... | collective-permute-start | bytes 1474568 | tf_op jit(solution)/shard_map/ppermute | solution.py:15
  13.7 54.6 %collective-permute-start.4 = (bf16[384,640]{1,0:T(8,128)(2,1)}, bf16[384,640]{1,0:T(8,128)(2,1)S(1)}, u32[]{:S(2)}, u32[]{:S(2)}) collective-permute-start(bf16[384,640]{1,0:T(8,128)(2,1)} %param.9), channel_id=1, source_target_pairs={{0,4},{4,8},{8,12},{1,5},{5,9},{9,13},{2,6},{6,10},{10,14},{3,7},{... | collective-permute-start | bytes 1474568 | tf_op jit(solution)/shard_map/ppermute | solution.py:15
  18.2 50.0 %collective-permute-start.5 = (bf16[384,640]{1,0:T(8,128)(2,1)}, bf16[384,640]{1,0:T(8,128)(2,1)S(1)}, u32[]{:S(2)}, u32[]{:S(2)}) collective-permute-start(bf16[384,640]{1,0:T(8,128)(2,1)} %param.9), channel_id=1, source_target_pairs={{4,0},{8,4},{12,8},{5,1},{9,5},{13,9},{6,2},{10,6},{14,10},{7,3},{... | collective-permute-start | bytes 1474568 | tf_op jit(solution)/shard_map/ppermute | solution.py:15
  19.5 27.6 %collective-permute-start = (s32[384]{0:T(512)}, s32[384]{0:T(512)S(1)}, u32[]{:S(2)}, u32[]{:S(2)}) collective-permute-start(s32[384]{0:T(512)} %param.12), channel_id=1, source_target_pairs={{0,4},{4,8},{8,12},{1,5},{5,9},{9,13},{2,6},{6,10},{10,14},{3,7},{... | collective-permute-start | bytes 4616 | tf_op jit(solution)/shard_map/ppermute | solution.py:15
  47.1 20.9 %collective-permute-start.1 = (s32[384]{0:T(512)}, s32[384]{0:T(512)S(1)}, u32[]{:S(2)}, u32[]{:S(2)}) collective-permute-start(s32[384]{0:T(512)} %param.12), channel_id=1, source_target_pairs={{4,0},{8,4},{12,8},{5,1},{9,5},{13,9},{6,2},{10,6},{14,10},{7,3},{... | collective-permute-start | bytes 4616 | tf_op jit(solution)/shard_map/ppermute | solution.py:15
  68.2 0.7 copy-start.2
  68.3 1.0 copy-start.3
  79.4 8.3 %collective-permute-start.6 = (bf16[384,640]{0,1:T(8,128)(2,1)S(1)}, bf16[384,640]{0,1:T(8,128)(2,1)S(1)}, u32[]{:S(2)}, u32[]{:S(2)}) collective-permute-start(bf16[384,640]{0,1:T(8,128)(2,1)S(1)} %get-tuple-element.28), channel_id=1, source_target_pairs={{0,1},{1,2},{2,3},{3,0},{4,5},{5,6},{6,7},{7,4},{8,9},{9,10},{10,1... | collective-permute-start | bytes 1474568 | tf_op jit(solution)/shard_map/ppermute | solution.py:84
  87.7 8.3 %collective-permute-start.7 = (bf16[384,640]{0,1:T(8,128)(2,1)S(1)}, bf16[384,640]{0,1:T(8,128)(2,1)S(1)}, u32[]{:S(2)}, u32[]{:S(2)}) collective-permute-start(bf16[384,640]{0,1:T(8,128)(2,1)S(1)} %collective-permute-done.6), channel_id=1, source_target_pairs={{0,1},{1,2},{2,3},{3,0},{4,5},{5,6},{6,7},{7,4},{8,9},{9,10},{10,1... | collective-permute-start | bytes 1474568 | tf_op jit(solution)/shard_map/ppermute | solution.py:84
  96.0 8.3 %collective-permute-start.8 = (bf16[384,640]{0,1:T(8,128)(2,1)S(1)}, bf16[384,640]{0,1:T(8,128)(2,1)S(1)}, u32[]{:S(2)}, u32[]{:S(2)}) collective-permute-start(bf16[384,640]{0,1:T(8,128)(2,1)S(1)} %collective-permute-done.7), channel_id=1, source_target_pairs={{0,1},{1,2},{2,3},{3,0},{4,5},{5,6},{6,7},{7,4},{8,9},{9,10},{10,1... | collective-permute-start | bytes 1474568 | tf_op jit(solution)/shard_map/ppermute | solution.py:84
Sparse Core Ops, SparseCore 0:
  8.9 135.7 all-gather.1
